TPU v7x, 256 devices: a whole 4x4x8 slice. The times are simulated.
256 devices in a mesh: seq: 32 (over x, z), tp: 8 (over y, core).
Axes of the slice: x: 4, y: 4, z: 8, core: 2. Of those that a mesh axis runs over, the one named last changes fastest.
Arguments:
- tokens: bfloat16 [32768, 2048], P('seq', 'tp'), may hold values from -6 to 6
- w_inner: bfloat16 [2048, 2, 4096], P('seq', None, 'tp'), may hold values from -0.125 to 0.125
- w_states: bfloat16 [2048, 256], P('seq'), may hold values from -0.125 to 0.125
- w_step: bfloat16 [2048, 64], P('seq', 'tp'), may hold values from -0.125 to 0.125
- conv_inner: float32 [4, 4096], P(None, 'tp'), may hold values from -3 to 3
- conv_states: float32 [4, 256], replicated, may hold values from -3 to 3
- decay_rate: float32 [64], P('tp'), may hold values from 0 to 1, as said below
- step_bias: float32 [64], P('tp'), may hold values from -1 to 0.5
- skip_gain: float32 [64], P('tp'), may hold values from 0.5 to 1.5
- norm_gain: float32 [4096], P('tp'), may hold values from 0.5 to 1.5
- w_output: bfloat16 [4096, 2048], P('tp', 'seq'), may hold values from -0.09375 to 0.09375
- block_owner: int32 [128], replicated, may hold values from 0 to 19, as said below
- lengths: int32 [20], replicated, may hold values from 1 to 16384, as said below
Outputs:
- mixed: bfloat16 [32768, 2048], P('seq', 'tp')
Inputs may be any that keep to these rules, and one draw needn't show every extreme that they name: `block_owner`: each prompt's blocks are consecutive, prompt r has ceil(lengths[r] / 256) of them, and the prompts follow one another in an order drawn afresh; one prompt has 64 blocks and is neither the first nor the last in that order. `lengths`: one prompt has exactly 16384 tokens. `decay_rate`: Positive.
All inputs are finite; a program needn't handle non-finite values.
Results may differ from a plain program's by a relative error of at most 0.0075.
Values may be sent and summed in bfloat16 or wider, within the bound.
No kernel may reach another device: no remote copies, remote signals or barrier semaphores. Data moves between devices by JAX's collectives and lax.ppermute only.
A program may use at most 64 MiB of HBM per device.

v0:
```python
import jax
import jax.numpy as jnp
from jax import lax
from jax.sharding import PartitionSpec as P

BLOCK = 256


def passed_along(value, axis, by):
    count = lax.axis_size(axis)
    pairs = [(i, i + by) for i in range(count) if 0 <= i + by < count]
    return lax.ppermute(value, axis, pairs)


def convolve(values, edge_rows, weights, in_block, carry_on):
    lag_rows = weights.shape[0] - 1
    row_total = values.shape[0]
    widened = jnp.concatenate([edge_rows, values], axis=0).astype(jnp.float32)
    total = jnp.zeros(values.shape, jnp.float32)
    for offset in range(weights.shape[0]):
        shifted = widened[lag_rows - offset : lag_rows - offset + row_total]
        keeping = (in_block >= offset) | carry_on
        total = total + jnp.where(keeping[:, None], shifted, 0.0) * weights[offset]
    return jax.nn.silu(total).astype(jnp.bfloat16)


def on_device(
    tokens,
    w_inner,
    w_states,
    w_step,
    conv_inner,
    conv_states,
    decay_rate,
    step_bias,
    skip_gain,
    norm_gain,
    w_output,
    block_owner,
    lengths,
):
    row_count = tokens.shape[0]
    local_blocks = row_count // BLOCK
    total_blocks = block_owner.shape[0]
    heads_here = w_step.shape[1]
    inner_here = w_inner.shape[2]
    state_size = w_states.shape[1] // 2
    head_size = inner_here // heads_here
    lag_rows = conv_inner.shape[0] - 1
    block_ids = jnp.arange(total_blocks, dtype=jnp.int32)
    same_owner = block_owner[:, None] == block_owner[None, :]
    first_block = jnp.min(jnp.where(same_owner, block_ids[None, :], total_blocks), axis=1)
    starting = (first_block == block_ids).astype(jnp.int32)
    request_ids = jnp.arange(lengths.shape[0], dtype=jnp.int32)
    own_length = jnp.sum(
        jnp.where(block_owner[:, None] == request_ids[None, :], lengths[None, :], 0), axis=1
    )
    valid_rows = jnp.clip(own_length - (block_ids - first_block) * BLOCK, 0, BLOCK)
    seq_index = lax.axis_index("seq")
    local_start = lax.dynamic_slice_in_dim(starting, seq_index * local_blocks, local_blocks)
    local_valid = lax.dynamic_slice_in_dim(valid_rows, seq_index * local_blocks, local_blocks)
    in_block = jnp.arange(row_count, dtype=jnp.int32) % BLOCK
    carry_on = jnp.repeat(local_start == 0, BLOCK)
    whole = lax.all_gather(tokens, "tp", axis=1, tiled=True)
    pieces = (
        lax.all_gather(w_inner, "seq", axis=0, tiled=True),
        lax.all_gather(w_states, "seq", axis=0, tiled=True),
        lax.all_gather(w_step, "seq", axis=0, tiled=True),
    )
    count = pieces[0].shape[0]
    inner_sum = jnp.dot(
        whole, pieces[0].reshape(count, 2 * inner_here), preferred_element_type=jnp.float32
    )
    states_sum = jnp.dot(whole, pieces[1], preferred_element_type=jnp.float32)
    step_sum = jnp.dot(whole, pieces[2], preferred_element_type=jnp.float32)
    projected = inner_sum.astype(jnp.bfloat16)
    gate_in = projected[:, :inner_here]
    x_in = projected[:, inner_here:]
    bc_in = states_sum.astype(jnp.bfloat16)
    step_raw = step_sum.astype(jnp.bfloat16)
    edge_inner, edge_states = passed_along(
        (x_in[row_count - lag_rows :], bc_in[row_count - lag_rows :]), "seq", 1
    )
    x_conv = convolve(x_in, edge_inner, conv_inner, in_block, carry_on)
    bc_conv = convolve(bc_in, edge_states, conv_states, in_block, carry_on)
    step_size = jax.nn.softplus(step_raw.astype(jnp.float32) + step_bias)
    log_decay = -decay_rate * step_size
    x_heads = x_conv.reshape(local_blocks, BLOCK, heads_here, head_size)
    b_rows = bc_conv[:, :state_size].reshape(local_blocks, BLOCK, state_size)
    c_rows = bc_conv[:, state_size:].reshape(local_blocks, BLOCK, state_size)
    step_blocks = step_size.reshape(local_blocks, BLOCK, heads_here)
    cumulative = jnp.cumsum(log_decay.reshape(local_blocks, BLOCK, heads_here), axis=1)
    causal = jnp.arange(BLOCK)[:, None] >= jnp.arange(BLOCK)[None, :]
    spread = cumulative[:, :, None, :] - cumulative[:, None, :, :]
    decays = jnp.exp(jnp.where(causal[None, :, :, None], spread, -jnp.inf))
    intersection = jnp.einsum("cin,cjn->cij", c_rows, b_rows, preferred_element_type=jnp.float32)
    mixing = (decays * intersection[:, :, :, None] * step_blocks[:, None, :, :]).astype(
        jnp.bfloat16
    )
    y_inner = jnp.einsum("cijh,cjhp->cihp", mixing, x_heads, preferred_element_type=jnp.float32)
    final_log = cumulative[:, -1, :]
    tail_weight = jnp.exp(final_log[:, None, :] - cumulative) * step_blocks
    weighted_b = (tail_weight[:, :, :, None] * b_rows.astype(jnp.float32)[:, :, None, :]).astype(
        jnp.bfloat16
    )
    fresh = jnp.einsum("cjhn,cjhp->chnp", weighted_b, x_heads, preferred_element_type=jnp.float32)
    keep_flag = jnp.where(local_start == 1, 0.0, 1.0).astype(jnp.float32)
    block_gain_each = jnp.exp(final_log) * keep_flag[:, None]

    def fold_block(carry, item):
        gain_now, fresh_now = item
        return ((carry[0] * gain_now, gain_now[:, None, None] * carry[1] + fresh_now), None)

    zero_state = jnp.zeros((heads_here, state_size, head_size), jnp.float32)
    unit_gain = jnp.ones((heads_here,), jnp.float32)
    (block_gain, block_state), _ = lax.scan(
        fold_block, (unit_gain, zero_state), (block_gain_each, fresh)
    )

    def relay(iteration, entering_now):
        return passed_along(block_gain[:, None, None] * entering_now + block_state, "seq", 1)

    entering = lax.fori_loop(0, lax.axis_size("seq") - 1, relay, zero_state)

    def pass_block(previous, item):
        log_now, keep_now, fresh_now = item
        incoming = previous * keep_now
        return (jnp.exp(log_now)[:, None, None] * incoming + fresh_now, incoming)

    _, incoming_all = lax.scan(pass_block, entering, (final_log, keep_flag, fresh))
    incoming_half = incoming_all.astype(jnp.bfloat16)
    y_carry = jnp.exp(cumulative)[:, :, :, None] * jnp.einsum(
        "cin,chnp->cihp", c_rows, incoming_half, preferred_element_type=jnp.float32
    )
    y_total = (y_inner + y_carry).reshape(row_count, inner_here) + jnp.repeat(skip_gain, head_size)[
        None, :
    ] * x_conv.astype(jnp.float32)
    gated = y_total * jax.nn.silu(gate_in.astype(jnp.float32))
    squares = lax.psum(jnp.sum(gated * gated, axis=1), "tp")
    square_mean = squares / (inner_here * lax.axis_size("tp"))
    normed = (gated * lax.rsqrt(square_mean + 1e-05)[:, None] * norm_gain).astype(jnp.bfloat16)
    partial_out = jnp.dot(
        normed,
        lax.all_gather(w_output, "seq", axis=1, tiled=True),
        preferred_element_type=jnp.float32,
    )
    summed = lax.psum_scatter(partial_out, "tp", scatter_dimension=1, tiled=True)
    live = in_block < jnp.repeat(local_valid, BLOCK)
    return jnp.where(live[:, None], summed, 0.0).astype(jnp.bfloat16)


def solution(mesh):
    return jax.shard_map(
        on_device,
        mesh=mesh,
        in_specs=(
            P("seq", "tp"),
            P("seq", None, "tp"),
            P("seq", None),
            P("seq", "tp"),
            P(None, "tp"),
            P(),
            P("tp"),
            P("tp"),
            P("tp"),
            P("tp"),
            P("tp", "seq"),
            P(),
            P(),
        ),
        out_specs=P("seq", "tp"),
        check_vma=False,
    )
```

profile of v0, /device:TPU:1, one launch (start us, length us, event | category | flops | bytes accessed | tf_op | source)
XLA Modules:
  0.0 875.8 jit_solution(9368195072958447139)
XLA Ops:
  13.4 41.9 %all-gather = bf16[32,64,8]{1,2,0:T(8,128)(2,1)S(1)} all-gather(bf16[1,64,8]{1,2,0:T(8,128)(2,1)} %bitcast.99), channel_id=1, replica_groups=mesh['seq'=32,'tp'=8] {'seq'}, dimensions={0}, use_global_device_ids=true | all-gather | bytes 33792 | tf_op jit(solution)/shard_map/all_gather | solution.py:68
  57.5 27.5 %all-gather.10.cloned.1.call-done = bf16[2048,256]{1,0:T(8,128)(2,1)} async-done(((bf16[64,256]{1,0:T(8,128)(2,1)}), bf16[2048,256]{1,0:T(8,128)(2,1)}) %all-gather.10.cloned.1.call-update) | async-done | bytes 1048592 | tf_op jit(solution)/shard_map/all_gather | solution.py:67
  85.0 42.9 %all-gather.6.cloned.1.call-done = bf16[1024,2048]{1,0:T(8,128)(2,1)} async-done(((bf16[1024,256]{1,0:T(8,128)(2,1)}), bf16[1024,2048]{1,0:T(8,128)(2,1)}) %all-gather.6.cloned.1.call-update) | async-done | bytes 4194320 | tf_op jit(solution)/shard_map/all_gather | solution.py:64
  141.9 67.3 %all-gather.8.cloned.1.call-done = bf16[2048,2,512]{2,1,0:T(2,128)(2,1)} async-done(((bf16[64,2,512]{2,1,0:T(2,128)(2,1)}), bf16[2048,2,512]{2,1,0:T(2,128)(2,1)}) %all-gather.8.cloned.1.call-update) | async-done | bytes 4194320 | tf_op jit(solution)/shard_map/all_gather | solution.py:66
  245.5 454.9 %while.35 = (s32[]{:T(128)}, f32[8,128,64]{2,1,0:T(8,128)S(1)}, f32[8]{0:T(128)S(1)}, f32[8,128,64]{2,1,0:T(8,128)S(1)}, s32[]{:T(128)}) while((s32[]{:T(128)}, f32[8,128,64]{2,1,0:T(8,128)S(1)}, f32[8]{0:T(128)S(1)}, f32[8,128,64]{2,1,0:T(8,128)S(1)}, s32[]{:T(128)}) %tuple.77), condition=%wide.region_7.8_spmd, body=%wide.region_6.7_spmd.sunk | while | flops 131074 | bytes 1835141 | solution.py:123
  249.8 7.4 collective-permute-done
  262.2 9.9 %collective-permute-done = f32[8,128,64]{2,1,0:T(8,128)S(1)} collective-permute-done((f32[8,128,64]{2,1,0:T(8,128)}, f32[8,128,64]{2,1,0:T(8,128)S(1)}, u32[]{:S(2)}, u32[]{:S(2)}) %collective-permute-start) | collective-permute-done | bytes 262176 | tf_op jit(solution)/shard_map/while/body/eval_jaxpr/ppermute | solution.py:12
  277.4 11.2 %collective-permute-done = f32[8,128,64]{2,1,0:T(8,128)S(1)} collective-permute-done((f32[8,128,64]{2,1,0:T(8,128)}, f32[8,128,64]{2,1,0:T(8,128)S(1)}, u32[]{:S(2)}, u32[]{:S(2)}) %collective-permute-start) | collective-permute-done | bytes 262176 | tf_op jit(solution)/shard_map/while/body/eval_jaxpr/ppermute | solution.py:12
  316.6 8.4 collective-permute-done
  329.6 9.5 %collective-permute-done = f32[8,128,64]{2,1,0:T(8,128)S(1)} collective-permute-done((f32[8,128,64]{2,1,0:T(8,128)}, f32[8,128,64]{2,1,0:T(8,128)S(1)}, u32[]{:S(2)}, u32[]{:S(2)}) %collective-permute-start) | collective-permute-done | bytes 262176 | tf_op jit(solution)/shard_map/while/body/eval_jaxpr/ppermute | solution.py:12
  343.8 10.7 %collective-permute-done = f32[8,128,64]{2,1,0:T(8,128)S(1)} collective-permute-done((f32[8,128,64]{2,1,0:T(8,128)}, f32[8,128,64]{2,1,0:T(8,128)S(1)}, u32[]{:S(2)}, u32[]{:S(2)}) %collective-permute-start) | collective-permute-done | bytes 262176 | tf_op jit(solution)/shard_map/while/body/eval_jaxpr/ppermute | solution.py:12
  359.2 11.8 %collective-permute-done = f32[8,128,64]{2,1,0:T(8,128)S(1)} collective-permute-done((f32[8,128,64]{2,1,0:T(8,128)}, f32[8,128,64]{2,1,0:T(8,128)S(1)}, u32[]{:S(2)}, u32[]{:S(2)}) %collective-permute-start) | collective-permute-done | bytes 262176 | tf_op jit(solution)/shard_map/while/body/eval_jaxpr/ppermute | solution.py:12
  376.7 12.0 %collective-permute-done = f32[8,128,64]{2,1,0:T(8,128)S(1)} collective-permute-done((f32[8,128,64]{2,1,0:T(8,128)}, f32[8,128,64]{2,1,0:T(8,128)S(1)}, u32[]{:S(2)}, u32[]{:S(2)}) %collective-permute-start) | collective-permute-done | bytes 262176 | tf_op jit(solution)/shard_map/while/body/eval_jaxpr/ppermute | solution.py:12
  394.9 10.9 %collective-permute-done = f32[8,128,64]{2,1,0:T(8,128)S(1)} collective-permute-done((f32[8,128,64]{2,1,0:T(8,128)}, f32[8,128,64]{2,1,0:T(8,128)S(1)}, u32[]{:S(2)}, u32[]{:S(2)}) %collective-permute-start) | collective-permute-done | bytes 262176 | tf_op jit(solution)/shard_map/while/body/eval_jaxpr/ppermute | solution.py:12
  411.4 9.8 %collective-permute-done = f32[8,128,64]{2,1,0:T(8,128)S(1)} collective-permute-done((f32[8,128,64]{2,1,0:T(8,128)}, f32[8,128,64]{2,1,0:T(8,128)S(1)}, u32[]{:S(2)}, u32[]{:S(2)}) %collective-permute-start) | collective-permute-done | bytes 262176 | tf_op jit(solution)/shard_map/while/body/eval_jaxpr/ppermute | solution.py:12
  426.1 8.6 collective-permute-done
  440.9 7.8 collective-permute-done
  519.0 8.3 collective-permute-done
  533.0 8.7 collective-permute-done
  548.7 9.5 %collective-permute-done = f32[8,128,64]{2,1,0:T(8,128)S(1)} collective-permute-done((f32[8,128,64]{2,1,0:T(8,128)}, f32[8,128,64]{2,1,0:T(8,128)S(1)}, u32[]{:S(2)}, u32[]{:S(2)}) %collective-permute-start) | collective-permute-done | bytes 262176 | tf_op jit(solution)/shard_map/while/body/eval_jaxpr/ppermute | solution.py:12
  566.1 10.6 %collective-permute-done = f32[8,128,64]{2,1,0:T(8,128)S(1)} collective-permute-done((f32[8,128,64]{2,1,0:T(8,128)}, f32[8,128,64]{2,1,0:T(8,128)S(1)}, u32[]{:S(2)}, u32[]{:S(2)}) %collective-permute-start) | collective-permute-done | bytes 262176 | tf_op jit(solution)/shard_map/while/body/eval_jaxpr/ppermute | solution.py:12
  577.7 7.6 collective-permute-start
  585.3 11.8 %collective-permute-done = f32[8,128,64]{2,1,0:T(8,128)S(1)} collective-permute-done((f32[8,128,64]{2,1,0:T(8,128)}, f32[8,128,64]{2,1,0:T(8,128)S(1)}, u32[]{:S(2)}, u32[]{:S(2)}) %collective-permute-start) | collective-permute-done | bytes 262176 | tf_op jit(solution)/shard_map/while/body/eval_jaxpr/ppermute | solution.py:12
  598.0 7.7 collective-permute-start
  605.7 11.1 %collective-permute-done = f32[8,128,64]{2,1,0:T(8,128)S(1)} collective-permute-done((f32[8,128,64]{2,1,0:T(8,128)}, f32[8,128,64]{2,1,0:T(8,128)S(1)}, u32[]{:S(2)}, u32[]{:S(2)}) %collective-permute-start) | collective-permute-done | bytes 262176 | tf_op jit(solution)/shard_map/while/body/eval_jaxpr/ppermute | solution.py:12
  624.5 9.9 %collective-permute-done = f32[8,128,64]{2,1,0:T(8,128)S(1)} collective-permute-done((f32[8,128,64]{2,1,0:T(8,128)}, f32[8,128,64]{2,1,0:T(8,128)S(1)}, u32[]{:S(2)}, u32[]{:S(2)}) %collective-permute-start) | collective-permute-done | bytes 262176 | tf_op jit(solution)/shard_map/while/body/eval_jaxpr/ppermute | solution.py:12
  641.4 8.8 %collective-permute-done = f32[8,128,64]{2,1,0:T(8,128)S(1)} collective-permute-done((f32[8,128,64]{2,1,0:T(8,128)}, f32[8,128,64]{2,1,0:T(8,128)S(1)}, u32[]{:S(2)}, u32[]{:S(2)}) %collective-permute-start) | collective-permute-done | bytes 262176 | tf_op jit(solution)/shard_map/while/body/eval_jaxpr/ppermute | solution.py:12
  656.4 7.6 collective-permute-done
  700.5 15.3 %while.36 = (s32[]{:T(128)}, f32[8,128,64]{2,1,0:T(8,128)S(1)}, bf16[4,8,128,64]{3,2,1,0:T(8,128)(2,1)}, f32[4,8]{1,0:T(4,128)S(1)}, f32[4]{0:T(128)S(1)}, /*index=5*/f32[4,8,128,64]{3,2,1,0:T(8,128)}, s32[]{:T(128)}) while((s32[]{:T(128)}, f32[8,128,64]{2,1,0:T(8,128)S(1)}, bf16[4,8,128,64]{3,2,1,0:T(8,128)(2,1)}, f32[4,8]{1,0:T(4,128)S(1)}, ...), condition=%wide.region_9.10_spmd, body=%wide.region_8.9_spmd.sunk | while | flops 262146 | bytes 1574085 | solution.py:130
  737.1 48.3 %psum.7 = f32[1024]{0:T(1024)S(1)} all-reduce(f32[1024]{0:T(1024)S(1)} %get-tuple-element.196), channel_id=1, replica_groups=mesh['seq'=32,'tp'=8] {'tp'}, use_global_device_ids=true, to_apply=%region_11.12 | all-reduce | flops 1024 | bytes 8192 | tf_op jit(solution)/shard_map/psum | solution.py:139
  785.4 7.9 fusion.26
  794.3 72.8 %reduce-scatter.2.cloned.1.call-done = f32[1024,256]{1,0:T(8,128)} async-done(((f32[1024,2048]{1,0:T(8,128)}), f32[1024,256]{1,0:T(8,128)}) %reduce-scatter.2.cloned.1.call-update) | async-done | bytes 1048592 | tf_op jit(solution)/shard_map/reduce_scatter | solution.py:147
  (212 shorter events, 340.8 us)
Async XLA Ops:
  6.5 78.4 %all-gather.10.cloned.1.call-start = ((), (), s32[]{:S(2)}) async-start(), calls=%async_computation.3 | async-start | bytes 1081344 | tf_op jit(solution)/shard_map/all_gather | solution.py:67
  7.3 120.7 %all-gather.6.cloned.1.call-start = ((), (), s32[]{:S(2)}) async-start(), calls=%async_computation.1 | async-start | bytes 4718592 | tf_op jit(solution)/shard_map/all_gather | solution.py:64
  8.0 201.3 %all-gather.8.cloned.1.call-start = ((), (), s32[]{:S(2)}) async-start(), calls=%async_computation.2 | async-start | bytes 4325376 | tf_op jit(solution)/shard_map/all_gather | solution.py:66
  8.7 776.7 %all-gather.12.cloned.1.call-start = ((), (), s32[]{:S(2)}) async-start(), calls=%async_computation.4 | async-start | bytes 2162688 | tf_op jit(solution)/shard_map/all_gather | solution.py:144
  9.3 857.7 %reduce-scatter.2.cloned.1.call-start = ((), (), s32[]{:S(2)}) async-start(), calls=%async_computation.5 | async-start | bytes 9437184 | tf_op jit(solution)/shard_map/reduce_scatter | solution.py:147
  258.1 14.0 %collective-permute-start = (f32[8,128,64]{2,1,0:T(8,128)}, f32[8,128,64]{2,1,0:T(8,128)S(1)}, u32[]{:S(2)}, u32[]{:S(2)}) collective-permute-start(f32[8,128,64]{2,1,0:T(8,128)} %multiply_add_fusion.2), channel_id=1, source_target_pairs={{0,8},{8,16},{16,24},{24,32},{32,40},{40,48},{48,56},{56,64},{64,7... | collective-permute-start | bytes 786440 | tf_op jit(solution)/shard_map/while/body/eval_jaxpr/ppermute | solution.py:12
  273.0 15.6 %collective-permute-start = (f32[8,128,64]{2,1,0:T(8,128)}, f32[8,128,64]{2,1,0:T(8,128)S(1)}, u32[]{:S(2)}, u32[]{:S(2)}) collective-permute-start(f32[8,128,64]{2,1,0:T(8,128)} %multiply_add_fusion.2), channel_id=1, source_target_pairs={{0,8},{8,16},{16,24},{24,32},{32,40},{40,48},{48,56},{56,64},{64,7... | collective-permute-start | bytes 786440 | tf_op jit(solution)/shard_map/while/body/eval_jaxpr/ppermute | solution.py:12
  312.9 12.1 %collective-permute-start = (f32[8,128,64]{2,1,0:T(8,128)}, f32[8,128,64]{2,1,0:T(8,128)S(1)}, u32[]{:S(2)}, u32[]{:S(2)}) collective-permute-start(f32[8,128,64]{2,1,0:T(8,128)} %multiply_add_fusion.2), channel_id=1, source_target_pairs={{0,8},{8,16},{16,24},{24,32},{32,40},{40,48},{48,56},{56,64},{64,7... | collective-permute-start | bytes 786440 | tf_op jit(solution)/shard_map/while/body/eval_jaxpr/ppermute | solution.py:12
  325.9 13.3 %collective-permute-start = (f32[8,128,64]{2,1,0:T(8,128)}, f32[8,128,64]{2,1,0:T(8,128)S(1)}, u32[]{:S(2)}, u32[]{:S(2)}) collective-permute-start(f32[8,128,64]{2,1,0:T(8,128)} %multiply_add_fusion.2), channel_id=1, source_target_pairs={{0,8},{8,16},{16,24},{24,32},{32,40},{40,48},{48,56},{56,64},{64,7... | collective-permute-start | bytes 786440 | tf_op jit(solution)/shard_map/while/body/eval_jaxpr/ppermute | solution.py:12
  340.1 14.4 %collective-permute-start = (f32[8,128,64]{2,1,0:T(8,128)}, f32[8,128,64]{2,1,0:T(8,128)S(1)}, u32[]{:S(2)}, u32[]{:S(2)}) collective-permute-start(f32[8,128,64]{2,1,0:T(8,128)} %multiply_add_fusion.2), channel_id=1, source_target_pairs={{0,8},{8,16},{16,24},{24,32},{32,40},{40,48},{48,56},{56,64},{64,7... | collective-permute-start | bytes 786440 | tf_op jit(solution)/shard_map/while/body/eval_jaxpr/ppermute | solution.py:12
  355.4 15.6 %collective-permute-start = (f32[8,128,64]{2,1,0:T(8,128)}, f32[8,128,64]{2,1,0:T(8,128)S(1)}, u32[]{:S(2)}, u32[]{:S(2)}) collective-permute-start(f32[8,128,64]{2,1,0:T(8,128)} %multiply_add_fusion.2), channel_id=1, source_target_pairs={{0,8},{8,16},{16,24},{24,32},{32,40},{40,48},{48,56},{56,64},{64,7... | collective-permute-start | bytes 786440 | tf_op jit(solution)/shard_map/while/body/eval_jaxpr/ppermute | solution.py:12
  371.9 16.8 %collective-permute-start = (f32[8,128,64]{2,1,0:T(8,128)}, f32[8,128,64]{2,1,0:T(8,128)S(1)}, u32[]{:S(2)}, u32[]{:S(2)}) collective-permute-start(f32[8,128,64]{2,1,0:T(8,128)} %multiply_add_fusion.2), channel_id=1, source_target_pairs={{0,8},{8,16},{16,24},{24,32},{32,40},{40,48},{48,56},{56,64},{64,7... | collective-permute-start | bytes 786440 | tf_op jit(solution)/shard_map/while/body/eval_jaxpr/ppermute | solution.py:12
  389.6 16.3 %collective-permute-start = (f32[8,128,64]{2,1,0:T(8,128)}, f32[8,128,64]{2,1,0:T(8,128)S(1)}, u32[]{:S(2)}, u32[]{:S(2)}) collective-permute-start(f32[8,128,64]{2,1,0:T(8,128)} %multiply_add_fusion.2), channel_id=1, source_target_pairs={{0,8},{8,16},{16,24},{24,32},{32,40},{40,48},{48,56},{56,64},{64,7... | collective-permute-start | bytes 786440 | tf_op jit(solution)/shard_map/while/body/eval_jaxpr/ppermute | solution.py:12
  406.7 14.4 %collective-permute-start = (f32[8,128,64]{2,1,0:T(8,128)}, f32[8,128,64]{2,1,0:T(8,128)S(1)}, u32[]{:S(2)}, u32[]{:S(2)}) collective-permute-start(f32[8,128,64]{2,1,0:T(8,128)} %multiply_add_fusion.2), channel_id=1, source_target_pairs={{0,8},{8,16},{16,24},{24,32},{32,40},{40,48},{48,56},{56,64},{64,7... | collective-permute-start | bytes 786440 | tf_op jit(solution)/shard_map/while/body/eval_jaxpr/ppermute | solution.py:12
  422.1 12.7 %collective-permute-start = (f32[8,128,64]{2,1,0:T(8,128)}, f32[8,128,64]{2,1,0:T(8,128)S(1)}, u32[]{:S(2)}, u32[]{:S(2)}) collective-permute-start(f32[8,128,64]{2,1,0:T(8,128)} %multiply_add_fusion.2), channel_id=1, source_target_pairs={{0,8},{8,16},{16,24},{24,32},{32,40},{40,48},{48,56},{56,64},{64,7... | collective-permute-start | bytes 786440 | tf_op jit(solution)/shard_map/while/body/eval_jaxpr/ppermute | solution.py:12
  435.7 13.0 %collective-permute-start = (f32[8,128,64]{2,1,0:T(8,128)}, f32[8,128,64]{2,1,0:T(8,128)S(1)}, u32[]{:S(2)}, u32[]{:S(2)}) collective-permute-start(f32[8,128,64]{2,1,0:T(8,128)} %multiply_add_fusion.2), channel_id=1, source_target_pairs={{0,8},{8,16},{16,24},{24,32},{32,40},{40,48},{48,56},{56,64},{64,7... | collective-permute-start | bytes 786440 | tf_op jit(solution)/shard_map/while/body/eval_jaxpr/ppermute | solution.py:12
  449.6 12.2 %collective-permute-start = (f32[8,128,64]{2,1,0:T(8,128)}, f32[8,128,64]{2,1,0:T(8,128)S(1)}, u32[]{:S(2)}, u32[]{:S(2)}) collective-permute-start(f32[8,128,64]{2,1,0:T(8,128)} %multiply_add_fusion.2), channel_id=1, source_target_pairs={{0,8},{8,16},{16,24},{24,32},{32,40},{40,48},{48,56},{56,64},{64,7... | collective-permute-start | bytes 786440 | tf_op jit(solution)/shard_map/while/body/eval_jaxpr/ppermute | solution.py:12
  462.7 11.6 %collective-permute-start = (f32[8,128,64]{2,1,0:T(8,128)}, f32[8,128,64]{2,1,0:T(8,128)S(1)}, u32[]{:S(2)}, u32[]{:S(2)}) collective-permute-start(f32[8,128,64]{2,1,0:T(8,128)} %multiply_add_fusion.2), channel_id=1, source_target_pairs={{0,8},{8,16},{16,24},{24,32},{32,40},{40,48},{48,56},{56,64},{64,7... | collective-permute-start | bytes 786440 | tf_op jit(solution)/shard_map/while/body/eval_jaxpr/ppermute | solution.py:12
  475.2 11.6 %collective-permute-start = (f32[8,128,64]{2,1,0:T(8,128)}, f32[8,128,64]{2,1,0:T(8,128)S(1)}, u32[]{:S(2)}, u32[]{:S(2)}) collective-permute-start(f32[8,128,64]{2,1,0:T(8,128)} %multiply_add_fusion.2), channel_id=1, source_target_pairs={{0,8},{8,16},{16,24},{24,32},{32,40},{40,48},{48,56},{56,64},{64,7... | collective-permute-start | bytes 786440 | tf_op jit(solution)/shard_map/while/body/eval_jaxpr/ppermute | solution.py:12
  487.7 11.6 %collective-permute-start = (f32[8,128,64]{2,1,0:T(8,128)}, f32[8,128,64]{2,1,0:T(8,128)S(1)}, u32[]{:S(2)}, u32[]{:S(2)}) collective-permute-start(f32[8,128,64]{2,1,0:T(8,128)} %multiply_add_fusion.2), channel_id=1, source_target_pairs={{0,8},{8,16},{16,24},{24,32},{32,40},{40,48},{48,56},{56,64},{64,7... | collective-permute-start | bytes 786440 | tf_op jit(solution)/shard_map/while/body/eval_jaxpr/ppermute | solution.py:12
  500.3 12.4 %collective-permute-start = (f32[8,128,64]{2,1,0:T(8,128)}, f32[8,128,64]{2,1,0:T(8,128)S(1)}, u32[]{:S(2)}, u32[]{:S(2)}) collective-permute-start(f32[8,128,64]{2,1,0:T(8,128)} %multiply_add_fusion.2), channel_id=1, source_target_pairs={{0,8},{8,16},{16,24},{24,32},{32,40},{40,48},{48,56},{56,64},{64,7... | collective-permute-start | bytes 786440 | tf_op jit(solution)/shard_map/while/body/eval_jaxpr/ppermute | solution.py:12
  513.5 13.7 %collective-permute-start = (f32[8,128,64]{2,1,0:T(8,128)}, f32[8,128,64]{2,1,0:T(8,128)S(1)}, u32[]{:S(2)}, u32[]{:S(2)}) collective-permute-start(f32[8,128,64]{2,1,0:T(8,128)} %multiply_add_fusion.2), channel_id=1, source_target_pairs={{0,8},{8,16},{16,24},{24,32},{32,40},{40,48},{48,56},{56,64},{64,7... | collective-permute-start | bytes 786440 | tf_op jit(solution)/shard_map/while/body/eval_jaxpr/ppermute | solution.py:12
  528.1 13.5 %collective-permute-start = (f32[8,128,64]{2,1,0:T(8,128)}, f32[8,128,64]{2,1,0:T(8,128)S(1)}, u32[]{:S(2)}, u32[]{:S(2)}) collective-permute-start(f32[8,128,64]{2,1,0:T(8,128)} %multiply_add_fusion.2), channel_id=1, source_target_pairs={{0,8},{8,16},{16,24},{24,32},{32,40},{40,48},{48,56},{56,64},{64,7... | collective-permute-start | bytes 786440 | tf_op jit(solution)/shard_map/while/body/eval_jaxpr/ppermute | solution.py:12
  542.5 15.6 %collective-permute-start = (f32[8,128,64]{2,1,0:T(8,128)}, f32[8,128,64]{2,1,0:T(8,128)S(1)}, u32[]{:S(2)}, u32[]{:S(2)}) collective-permute-start(f32[8,128,64]{2,1,0:T(8,128)} %multiply_add_fusion.2), channel_id=1, source_target_pairs={{0,8},{8,16},{16,24},{24,32},{32,40},{40,48},{48,56},{56,64},{64,7... | collective-permute-start | bytes 786440 | tf_op jit(solution)/shard_map/while/body/eval_jaxpr/ppermute | solution.py:12
  559.1 17.7 %collective-permute-start = (f32[8,128,64]{2,1,0:T(8,128)}, f32[8,128,64]{2,1,0:T(8,128)S(1)}, u32[]{:S(2)}, u32[]{:S(2)}) collective-permute-start(f32[8,128,64]{2,1,0:T(8,128)} %multiply_add_fusion.2), channel_id=1, source_target_pairs={{0,8},{8,16},{16,24},{24,32},{32,40},{40,48},{48,56},{56,64},{64,7... | collective-permute-start | bytes 786440 | tf_op jit(solution)/shard_map/while/body/eval_jaxpr/ppermute | solution.py:12
  577.7 19.4 %collective-permute-start = (f32[8,128,64]{2,1,0:T(8,128)}, f32[8,128,64]{2,1,0:T(8,128)S(1)}, u32[]{:S(2)}, u32[]{:S(2)}) collective-permute-start(f32[8,128,64]{2,1,0:T(8,128)} %multiply_add_fusion.2), channel_id=1, source_target_pairs={{0,8},{8,16},{16,24},{24,32},{32,40},{40,48},{48,56},{56,64},{64,7... | collective-permute-start | bytes 786440 | tf_op jit(solution)/shard_map/while/body/eval_jaxpr/ppermute | solution.py:12
  598.0 18.8 %collective-permute-start = (f32[8,128,64]{2,1,0:T(8,128)}, f32[8,128,64]{2,1,0:T(8,128)S(1)}, u32[]{:S(2)}, u32[]{:S(2)}) collective-permute-start(f32[8,128,64]{2,1,0:T(8,128)} %multiply_add_fusion.2), channel_id=1, source_target_pairs={{0,8},{8,16},{16,24},{24,32},{32,40},{40,48},{48,56},{56,64},{64,7... | collective-permute-start | bytes 786440 | tf_op jit(solution)/shard_map/while/body/eval_jaxpr/ppermute | solution.py:12
  617.7 16.6 %collective-permute-start = (f32[8,128,64]{2,1,0:T(8,128)}, f32[8,128,64]{2,1,0:T(8,128)S(1)}, u32[]{:S(2)}, u32[]{:S(2)}) collective-permute-start(f32[8,128,64]{2,1,0:T(8,128)} %multiply_add_fusion.2), channel_id=1, source_target_pairs={{0,8},{8,16},{16,24},{24,32},{32,40},{40,48},{48,56},{56,64},{64,7... | collective-permute-start | bytes 786440 | tf_op jit(solution)/shard_map/while/body/eval_jaxpr/ppermute | solution.py:12
  635.3 14.9 %collective-permute-start = (f32[8,128,64]{2,1,0:T(8,128)}, f32[8,128,64]{2,1,0:T(8,128)S(1)}, u32[]{:S(2)}, u32[]{:S(2)}) collective-permute-start(f32[8,128,64]{2,1,0:T(8,128)} %multiply_add_fusion.2), channel_id=1, source_target_pairs={{0,8},{8,16},{16,24},{24,32},{32,40},{40,48},{48,56},{56,64},{64,7... | collective-permute-start | bytes 786440 | tf_op jit(solution)/shard_map/while/body/eval_jaxpr/ppermute | solution.py:12
  651.1 12.9 %collective-permute-start = (f32[8,128,64]{2,1,0:T(8,128)}, f32[8,128,64]{2,1,0:T(8,128)S(1)}, u32[]{:S(2)}, u32[]{:S(2)}) collective-permute-start(f32[8,128,64]{2,1,0:T(8,128)} %multiply_add_fusion.2), channel_id=1, source_target_pairs={{0,8},{8,16},{16,24},{24,32},{32,40},{40,48},{48,56},{56,64},{64,7... | collective-permute-start | bytes 786440 | tf_op jit(solution)/shard_map/while/body/eval_jaxpr/ppermute | solution.py:12
  676.6 11.6 %collective-permute-start = (f32[8,128,64]{2,1,0:T(8,128)}, f32[8,128,64]{2,1,0:T(8,128)S(1)}, u32[]{:S(2)}, u32[]{:S(2)}) collective-permute-start(f32[8,128,64]{2,1,0:T(8,128)} %multiply_add_fusion.2), channel_id=1, source_target_pairs={{0,8},{8,16},{16,24},{24,32},{32,40},{40,48},{48,56},{56,64},{64,7... | collective-permute-start | bytes 786440 | tf_op jit(solution)/shard_map/while/body/eval_jaxpr/ppermute | solution.py:12
  689.1 11.4 %collective-permute-start = (f32[8,128,64]{2,1,0:T(8,128)}, f32[8,128,64]{2,1,0:T(8,128)S(1)}, u32[]{:S(2)}, u32[]{:S(2)}) collective-permute-start(f32[8,128,64]{2,1,0:T(8,128)} %multiply_add_fusion.2), channel_id=1, source_target_pairs={{0,8},{8,16},{16,24},{24,32},{32,40},{40,48},{48,56},{56,64},{64,7... | collective-permute-start | bytes 786440 | tf_op jit(solution)/shard_map/while/body/eval_jaxpr/ppermute | solution.py:12
  (27 other events, 1237.1 us)
Sparse Core Ops, SparseCore 0:
  9.9 75.0 all-gather.9
  86.8 41.0 all-gather.5
  130.5 78.7 all-gather.7
  211.7 75.2 all-gather.11
  793.5 73.4 reduce-scatter.1
where the time goes:
time: 878 us; the launch traced here: 876 us
  waiting for transfers between devices  483 us (55%)
  starting transfers between devices  162 us (18%)
  blocking collectives  90.2 us (10%)
  other arithmetic  68 us (8%)
  local copies, waits for them, and re-layouts  29.4 us (3%)
  matrix products  28.5 us (3%)
  between operations  13.5 us (2%)
    ppermute x33, waiting for transfers between devices, passed_along(): return lax.ppermute(value, axis, pairs)  270 us
    ppermute x33, starting transfers between devices, passed_along(): return lax.ppermute(value, axis, pairs)  162 us
    reduce_scatter x1, waiting for transfers between devices, on_device(): lax.psum_scatter(partial_out, 'tp', scatter_dimension=1, tiled=True)  72.8 us
    all_gather x1, waiting for transfers between devices, on_device(): lax.all_gather(w_inner, 'seq', axis=0, tiled=True)  67.3 us
    psum x1, blocking collectives, on_device(): squares = lax.psum(jnp.sum(gated * gated, axis=1), 'tp')  48.3 us
    all_gather x1, waiting for transfers between devices, on_device(): whole = lax.all_gather(tokens, 'tp', axis=1, tiled=True)  42.9 us
    all_gather x1, blocking collectives, on_device(): lax.all_gather(w_step, 'seq', axis=0, tiled=True)  41.9 us
    add x31, other arithmetic, relay(): block_gain[:, None, None] * entering_now + block_state  28.2 us
  transfers between devices with their start and end apart: 38, of which 35 were waited for; matrix products, arithmetic and copies ran while one was open for 13% of the time, Pallas kernels for 0%

commit v1 on v0

--- a/solution.py
+++ b/solution.py
@@ -1,9 +1,20 @@
+import functools
 import jax
 import jax.numpy as jnp
 from jax import lax
 from jax.sharding import PartitionSpec as P
 
 BLOCK = 256
+
+
+def _connect_layers_all(patch, in_dim):
+    cores_n = jax.lax.axis_size("tp")
+    step_out = jnp.tile(patch, [cores_n if jj == in_dim else 1 for jj in range(patch.ndim)])
+    s_next = jax.lax.all_to_all(step_out, "tp", split_axis=in_dim, concat_axis=in_dim, tiled=True)
+    return s_next
+
+
+_remake_views = functools.partial(_connect_layers_all, in_dim=1)
 
 
 def passed_along(value, axis, by):
@@ -61,7 +72,7 @@
     local_valid = lax.dynamic_slice_in_dim(valid_rows, seq_index * local_blocks, local_blocks)
     in_block = jnp.arange(row_count, dtype=jnp.int32) % BLOCK
     carry_on = jnp.repeat(local_start == 0, BLOCK)
-    whole = lax.all_gather(tokens, "tp", axis=1, tiled=True)
+    whole = _remake_views(tokens)
     pieces = (
         lax.all_gather(w_inner, "seq", axis=0, tiled=True),
         lax.all_gather(w_states, "seq", axis=0, tiled=True),

time: 878 us -> 838 us (0.954)
  waiting for transfers between devices: 483 us -> 429 us
  starting transfers between devices: 162 us -> 172 us
    all_gather x1 -> x0, waiting for transfers between devices: 42.9 us -> none  [on_device(): whole = lax.all_gather(tokens, 'tp', axis=1, tiled=True)]
    all_gather x1, waiting for transfers between devices: 27.5 us -> 11.1 us  [on_device(): lax.all_gather(w_states, 'seq', axis=0, tiled=True)]
  transfers between devices with their start and end apart: 38 -> 38, of which waited for: 35 -> 35; matrix products, arithmetic and copies ran while one was open for 13% -> 14% of each run, Pallas kernels for 0% -> 0%
where the time goes in v1:
time: 838 us; the launch traced here: 835 us
  waiting for transfers between devices  429 us (51%)
  starting transfers between devices  172 us (21%)
  blocking collectives  89.6 us (11%)
  other arithmetic  66.6 us (8%)
  local copies, waits for them, and re-layouts  36.4 us (4%)
  matrix products  28 us (3%)
  between operations  13.6 us (2%)
    ppermute x33, waiting for transfers between devices, passed_along(): return lax.ppermute(value, axis, pairs)  269 us
    ppermute x33, starting transfers between devices, passed_along(): return lax.ppermute(value, axis, pairs)  164 us
    reduce_scatter x1, waiting for transfers between devices, on_device(): lax.psum_scatter(partial_out, 'tp', scatter_dimension=1, tiled=True)  72.1 us
    all_gather x1, waiting for transfers between devices, on_device(): lax.all_gather(w_inner, 'seq', axis=0, tiled=True)  70.5 us
    psum x1, blocking collectives, on_device(): squares = lax.psum(jnp.sum(gated * gated, axis=1), 'tp')  47.7 us
    all_gather x1, blocking collectives, on_device(): lax.all_gather(w_step, 'seq', axis=0, tiled=True)  41.9 us
    add x31, other arithmetic, relay(): block_gain[:, None, None] * entering_now + block_state  28.2 us
  transfers between devices with their start and end apart: 38, of which 35 were waited for; matrix products, arithmetic and copies ran while one was open for 14% of the time, Pallas kernels for 0%

profile of v1, /device:TPU:1, one launch (start us, length us, event | category | flops | bytes accessed | tf_op | source)
XLA Modules:
  0.0 835.3 jit_solution(4307910220471223635)
XLA Ops:
  11.3 7.8 all-to-all-start
  20.3 41.9 %all-gather = bf16[32,64,8]{1,2,0:T(8,128)(2,1)S(1)} all-gather(bf16[1,64,8]{1,2,0:T(8,128)(2,1)S(1)} %bitcast.103), channel_id=1, replica_groups=mesh['seq'=32,'tp'=8] {'seq'}, dimensions={0}, use_global_device_ids=true | all-gather | bytes 33792 | tf_op jit(solution)/shard_map/all_gather | solution.py:79
  74.4 11.1 %all-gather.7.cloned.1.call-done = bf16[2048,256]{1,0:T(8,128)(2,1)} async-done(((bf16[64,256]{1,0:T(8,128)(2,1)}), bf16[2048,256]{1,0:T(8,128)(2,1)}) %all-gather.7.cloned.1.call-update) | async-done | bytes 1048592 | tf_op jit(solution)/shard_map/all_gather | solution.py:78
  98.0 70.5 %all-gather.5.cloned.1.call-done = bf16[2048,2,512]{2,1,0:T(2,128)(2,1)} async-done(((bf16[64,2,512]{2,1,0:T(2,128)(2,1)}), bf16[2048,2,512]{2,1,0:T(2,128)(2,1)}) %all-gather.5.cloned.1.call-update) | async-done | bytes 4194320 | tf_op jit(solution)/shard_map/all_gather | solution.py:77
  204.6 456.6 %while.35 = (s32[]{:T(128)}, f32[8,128,64]{2,1,0:T(8,128)S(1)}, f32[8]{0:T(128)S(1)}, f32[8,128,64]{2,1,0:T(8,128)S(1)}, s32[]{:T(128)}) while((s32[]{:T(128)}, f32[8,128,64]{2,1,0:T(8,128)S(1)}, f32[8]{0:T(128)S(1)}, f32[8,128,64]{2,1,0:T(8,128)S(1)}, s32[]{:T(128)}) %tuple.79), condition=%wide.region_7.8_spmd, body=%wide.region_6.7_spmd.sunk | while | flops 131074 | bytes 1835141 | solution.py:134
  208.9 7.4 collective-permute-done
  221.3 10.2 %collective-permute-done = f32[8,128,64]{2,1,0:T(8,128)S(1)} collective-permute-done((f32[8,128,64]{2,1,0:T(8,128)}, f32[8,128,64]{2,1,0:T(8,128)S(1)}, u32[]{:S(2)}, u32[]{:S(2)}) %collective-permute-start) | collective-permute-done | bytes 262176 | tf_op jit(solution)/shard_map/while/body/eval_jaxpr/ppermute | solution.py:23
  237.2 11.4 %collective-permute-done = f32[8,128,64]{2,1,0:T(8,128)S(1)} collective-permute-done((f32[8,128,64]{2,1,0:T(8,128)}, f32[8,128,64]{2,1,0:T(8,128)S(1)}, u32[]{:S(2)}, u32[]{:S(2)}) %collective-permute-start) | collective-permute-done | bytes 262176 | tf_op jit(solution)/shard_map/while/body/eval_jaxpr/ppermute | solution.py:23
  276.0 7.3 collective-permute-done
  288.0 8.5 %collective-permute-done = f32[8,128,64]{2,1,0:T(8,128)S(1)} collective-permute-done((f32[8,128,64]{2,1,0:T(8,128)}, f32[8,128,64]{2,1,0:T(8,128)S(1)}, u32[]{:S(2)}, u32[]{:S(2)}) %collective-permute-start) | collective-permute-done | bytes 262176 | tf_op jit(solution)/shard_map/while/body/eval_jaxpr/ppermute | solution.py:23
  303.3 10.1 %collective-permute-done = f32[8,128,64]{2,1,0:T(8,128)S(1)} collective-permute-done((f32[8,128,64]{2,1,0:T(8,128)}, f32[8,128,64]{2,1,0:T(8,128)S(1)}, u32[]{:S(2)}, u32[]{:S(2)}) %collective-permute-start) | collective-permute-done | bytes 262176 | tf_op jit(solution)/shard_map/while/body/eval_jaxpr/ppermute | solution.py:23
  320.1 11.2 %collective-permute-done = f32[8,128,64]{2,1,0:T(8,128)S(1)} collective-permute-done((f32[8,128,64]{2,1,0:T(8,128)}, f32[8,128,64]{2,1,0:T(8,128)S(1)}, u32[]{:S(2)}, u32[]{:S(2)}) %collective-permute-start) | collective-permute-done | bytes 262176 | tf_op jit(solution)/shard_map/while/body/eval_jaxpr/ppermute | solution.py:23
  338.1 11.6 %collective-permute-done = f32[8,128,64]{2,1,0:T(8,128)S(1)} collective-permute-done((f32[8,128,64]{2,1,0:T(8,128)}, f32[8,128,64]{2,1,0:T(8,128)S(1)}, u32[]{:S(2)}, u32[]{:S(2)}) %collective-permute-start) | collective-permute-done | bytes 262176 | tf_op jit(solution)/shard_map/while/body/eval_jaxpr/ppermute | solution.py:23
  355.9 10.5 %collective-permute-done = f32[8,128,64]{2,1,0:T(8,128)S(1)} collective-permute-done((f32[8,128,64]{2,1,0:T(8,128)}, f32[8,128,64]{2,1,0:T(8,128)S(1)}, u32[]{:S(2)}, u32[]{:S(2)}) %collective-permute-start) | collective-permute-done | bytes 262176 | tf_op jit(solution)/shard_map/while/body/eval_jaxpr/ppermute | solution.py:23
  371.6 9.3 %collective-permute-done = f32[8,128,64]{2,1,0:T(8,128)S(1)} collective-permute-done((f32[8,128,64]{2,1,0:T(8,128)}, f32[8,128,64]{2,1,0:T(8,128)S(1)}, u32[]{:S(2)}, u32[]{:S(2)}) %collective-permute-start) | collective-permute-done | bytes 262176 | tf_op jit(solution)/shard_map/while/body/eval_jaxpr/ppermute | solution.py:23
  387.1 8.4 %collective-permute-done = f32[8,128,64]{2,1,0:T(8,128)S(1)} collective-permute-done((f32[8,128,64]{2,1,0:T(8,128)}, f32[8,128,64]{2,1,0:T(8,128)S(1)}, u32[]{:S(2)}, u32[]{:S(2)}) %collective-permute-start) | collective-permute-done | bytes 262176 | tf_op jit(solution)/shard_map/while/body/eval_jaxpr/ppermute | solution.py:23
  401.7 7.6 collective-permute-done
  479.7 8.4 %collective-permute-done = f32[8,128,64]{2,1,0:T(8,128)S(1)} collective-permute-done((f32[8,128,64]{2,1,0:T(8,128)}, f32[8,128,64]{2,1,0:T(8,128)S(1)}, u32[]{:S(2)}, u32[]{:S(2)}) %collective-permute-start) | collective-permute-done | bytes 262176 | tf_op jit(solution)/shard_map/while/body/eval_jaxpr/ppermute | solution.py:23
  494.8 9.5 %collective-permute-done = f32[8,128,64]{2,1,0:T(8,128)S(1)} collective-permute-done((f32[8,128,64]{2,1,0:T(8,128)}, f32[8,128,64]{2,1,0:T(8,128)S(1)}, u32[]{:S(2)}, u32[]{:S(2)}) %collective-permute-start) | collective-permute-done | bytes 262176 | tf_op jit(solution)/shard_map/while/body/eval_jaxpr/ppermute | solution.py:23
  509.9 10.1 %collective-permute-done = f32[8,128,64]{2,1,0:T(8,128)S(1)} collective-permute-done((f32[8,128,64]{2,1,0:T(8,128)}, f32[8,128,64]{2,1,0:T(8,128)S(1)}, u32[]{:S(2)}, u32[]{:S(2)}) %collective-permute-start) | collective-permute-done | bytes 262176 | tf_op jit(solution)/shard_map/while/body/eval_jaxpr/ppermute | solution.py:23
  526.0 10.8 %collective-permute-done = f32[8,128,64]{2,1,0:T(8,128)S(1)} collective-permute-done((f32[8,128,64]{2,1,0:T(8,128)}, f32[8,128,64]{2,1,0:T(8,128)S(1)}, u32[]{:S(2)}, u32[]{:S(2)}) %collective-permute-start) | collective-permute-done | bytes 262176 | tf_op jit(solution)/shard_map/while/body/eval_jaxpr/ppermute | solution.py:23
  542.1 11.3 %collective-permute-done = f32[8,128,64]{2,1,0:T(8,128)S(1)} collective-permute-done((f32[8,128,64]{2,1,0:T(8,128)}, f32[8,128,64]{2,1,0:T(8,128)S(1)}, u32[]{:S(2)}, u32[]{:S(2)}) %collective-permute-start) | collective-permute-done | bytes 262176 | tf_op jit(solution)/shard_map/while/body/eval_jaxpr/ppermute | solution.py:23
  554.4 7.3 collective-permute-start
  561.7 11.6 %collective-permute-done = f32[8,128,64]{2,1,0:T(8,128)S(1)} collective-permute-done((f32[8,128,64]{2,1,0:T(8,128)}, f32[8,128,64]{2,1,0:T(8,128)S(1)}, u32[]{:S(2)}, u32[]{:S(2)}) %collective-permute-start) | collective-permute-done | bytes 262176 | tf_op jit(solution)/shard_map/while/body/eval_jaxpr/ppermute | solution.py:23
  574.2 7.3 collective-permute-start
  581.6 10.5 %collective-permute-done = f32[8,128,64]{2,1,0:T(8,128)S(1)} collective-permute-done((f32[8,128,64]{2,1,0:T(8,128)}, f32[8,128,64]{2,1,0:T(8,128)S(1)}, u32[]{:S(2)}, u32[]{:S(2)}) %collective-permute-start) | collective-permute-done | bytes 262176 | tf_op jit(solution)/shard_map/while/body/eval_jaxpr/ppermute | solution.py:23
  599.5 9.3 %collective-permute-done = f32[8,128,64]{2,1,0:T(8,128)S(1)} collective-permute-done((f32[8,128,64]{2,1,0:T(8,128)}, f32[8,128,64]{2,1,0:T(8,128)S(1)}, u32[]{:S(2)}, u32[]{:S(2)}) %collective-permute-start) | collective-permute-done | bytes 262176 | tf_op jit(solution)/shard_map/while/body/eval_jaxpr/ppermute | solution.py:23
  615.3 8.2 collective-permute-done
  661.2 15.3 %while.36 = (s32[]{:T(128)}, f32[8,128,64]{2,1,0:T(8,128)S(1)}, bf16[4,8,128,64]{3,2,1,0:T(8,128)(2,1)}, f32[4,8]{1,0:T(4,128)S(1)}, f32[4]{0:T(128)S(1)}, /*index=5*/f32[4,8,128,64]{3,2,1,0:T(8,128)}, s32[]{:T(128)}) while((s32[]{:T(128)}, f32[8,128,64]{2,1,0:T(8,128)S(1)}, bf16[4,8,128,64]{3,2,1,0:T(8,128)(2,1)}, f32[4,8]{1,0:T(4,128)S(1)}, ...), condition=%wide.region_9.10_spmd, body=%wide.region_8.9_spmd.sunk | while | flops 262146 | bytes 1574085 | solution.py:141
  697.9 47.7 %psum.7 = f32[1024]{0:T(1024)S(1)} all-reduce(f32[1024]{0:T(1024)S(1)} %get-tuple-element.207), channel_id=1, replica_groups=mesh['seq'=32,'tp'=8] {'tp'}, use_global_device_ids=true, to_apply=%region_11.12 | all-reduce | flops 1024 | bytes 8192 | tf_op jit(solution)/shard_map/psum | solution.py:150
  745.7 7.9 fusion.26
  754.5 72.1 %reduce-scatter.2.cloned.1.call-done = f32[1024,256]{1,0:T(8,128)} async-done(((f32[1024,2048]{1,0:T(8,128)}), f32[1024,256]{1,0:T(8,128)}) %reduce-scatter.2.cloned.1.call-update) | async-done | bytes 1048592 | tf_op jit(solution)/shard_map/reduce_scatter | solution.py:158
  (225 shorter events, 351.5 us)
Async XLA Ops:
  6.5 78.9 %all-gather.7.cloned.1.call-start = ((), (), s32[]{:S(2)}) async-start(), calls=%async_computation.3 | async-start | bytes 1081344 | tf_op jit(solution)/shard_map/all_gather | solution.py:78
  7.3 161.2 %all-gather.5.cloned.1.call-start = ((), (), s32[]{:S(2)}) async-start(), calls=%async_computation.2 | async-start | bytes 4325376 | tf_op jit(solution)/shard_map/all_gather | solution.py:77
  11.3 56.6 %all-to-all-start = ((bf16[1024,8,256]{2,0,1:T(8,128)(2,1)}), bf16[1024,8,256]{2,0,1:T(8,128)(2,1)}, u32[]{:S(2)}, u32[]{:S(2)}) async-start(bf16[1024,8,256]{2,0,1:T(8,128)(2,1)} %tile.2), calls=%async_computation | async-start | bytes 8388608 | tf_op jit(solution)/shard_map/all_to_all | solution.py:13
  19.1 726.5 %all-gather.9.cloned.1.call-start = ((), (), s32[]{:S(2)}) async-start(), calls=%async_computation.4 | async-start | bytes 2162688 | tf_op jit(solution)/shard_map/all_gather | solution.py:155
  19.9 806.7 %reduce-scatter.2.cloned.1.call-start = ((), (), s32[]{:S(2)}) async-start(), calls=%async_computation.5 | async-start | bytes 9437184 | tf_op jit(solution)/shard_map/reduce_scatter | solution.py:158
  217.2 14.2 %collective-permute-start = (f32[8,128,64]{2,1,0:T(8,128)}, f32[8,128,64]{2,1,0:T(8,128)S(1)}, u32[]{:S(2)}, u32[]{:S(2)}) collective-permute-start(f32[8,128,64]{2,1,0:T(8,128)} %multiply_add_fusion.2), channel_id=1, source_target_pairs={{0,8},{8,16},{16,24},{24,32},{32,40},{40,48},{48,56},{56,64},{64,7... | collective-permute-start | bytes 786440 | tf_op jit(solution)/shard_map/while/body/eval_jaxpr/ppermute | solution.py:23
  232.3 16.3 %collective-permute-start = (f32[8,128,64]{2,1,0:T(8,128)}, f32[8,128,64]{2,1,0:T(8,128)S(1)}, u32[]{:S(2)}, u32[]{:S(2)}) collective-permute-start(f32[8,128,64]{2,1,0:T(8,128)} %multiply_add_fusion.2), channel_id=1, source_target_pairs={{0,8},{8,16},{16,24},{24,32},{32,40},{40,48},{48,56},{56,64},{64,7... | collective-permute-start | bytes 786440 | tf_op jit(solution)/shard_map/while/body/eval_jaxpr/ppermute | solution.py:23
  284.3 12.2 %collective-permute-start = (f32[8,128,64]{2,1,0:T(8,128)}, f32[8,128,64]{2,1,0:T(8,128)S(1)}, u32[]{:S(2)}, u32[]{:S(2)}) collective-permute-start(f32[8,128,64]{2,1,0:T(8,128)} %multiply_add_fusion.2), channel_id=1, source_target_pairs={{0,8},{8,16},{16,24},{24,32},{32,40},{40,48},{48,56},{56,64},{64,7... | collective-permute-start | bytes 786440 | tf_op jit(solution)/shard_map/while/body/eval_jaxpr/ppermute | solution.py:23
  297.4 16.0 %collective-permute-start = (f32[8,128,64]{2,1,0:T(8,128)}, f32[8,128,64]{2,1,0:T(8,128)S(1)}, u32[]{:S(2)}, u32[]{:S(2)}) collective-permute-start(f32[8,128,64]{2,1,0:T(8,128)} %multiply_add_fusion.2), channel_id=1, source_target_pairs={{0,8},{8,16},{16,24},{24,32},{32,40},{40,48},{48,56},{56,64},{64,7... | collective-permute-start | bytes 786440 | tf_op jit(solution)/shard_map/while/body/eval_jaxpr/ppermute | solution.py:23
  314.3 17.1 %collective-permute-start = (f32[8,128,64]{2,1,0:T(8,128)}, f32[8,128,64]{2,1,0:T(8,128)S(1)}, u32[]{:S(2)}, u32[]{:S(2)}) collective-permute-start(f32[8,128,64]{2,1,0:T(8,128)} %multiply_add_fusion.2), channel_id=1, source_target_pairs={{0,8},{8,16},{16,24},{24,32},{32,40},{40,48},{48,56},{56,64},{64,7... | collective-permute-start | bytes 786440 | tf_op jit(solution)/shard_map/while/body/eval_jaxpr/ppermute | solution.py:23
  332.3 17.5 %collective-permute-start = (f32[8,128,64]{2,1,0:T(8,128)}, f32[8,128,64]{2,1,0:T(8,128)S(1)}, u32[]{:S(2)}, u32[]{:S(2)}) collective-permute-start(f32[8,128,64]{2,1,0:T(8,128)} %multiply_add_fusion.2), channel_id=1, source_target_pairs={{0,8},{8,16},{16,24},{24,32},{32,40},{40,48},{48,56},{56,64},{64,7... | collective-permute-start | bytes 786440 | tf_op jit(solution)/shard_map/while/body/eval_jaxpr/ppermute | solution.py:23
  350.6 15.7 %collective-permute-start = (f32[8,128,64]{2,1,0:T(8,128)}, f32[8,128,64]{2,1,0:T(8,128)S(1)}, u32[]{:S(2)}, u32[]{:S(2)}) collective-permute-start(f32[8,128,64]{2,1,0:T(8,128)} %multiply_add_fusion.2), channel_id=1, source_target_pairs={{0,8},{8,16},{16,24},{24,32},{32,40},{40,48},{48,56},{56,64},{64,7... | collective-permute-start | bytes 786440 | tf_op jit(solution)/shard_map/while/body/eval_jaxpr/ppermute | solution.py:23
  367.2 13.7 %collective-permute-start = (f32[8,128,64]{2,1,0:T(8,128)}, f32[8,128,64]{2,1,0:T(8,128)S(1)}, u32[]{:S(2)}, u32[]{:S(2)}) collective-permute-start(f32[8,128,64]{2,1,0:T(8,128)} %multiply_add_fusion.2), channel_id=1, source_target_pairs={{0,8},{8,16},{16,24},{24,32},{32,40},{40,48},{48,56},{56,64},{64,7... | collective-permute-start | bytes 786440 | tf_op jit(solution)/shard_map/while/body/eval_jaxpr/ppermute | solution.py:23
  381.8 13.7 %collective-permute-start = (f32[8,128,64]{2,1,0:T(8,128)}, f32[8,128,64]{2,1,0:T(8,128)S(1)}, u32[]{:S(2)}, u32[]{:S(2)}) collective-permute-start(f32[8,128,64]{2,1,0:T(8,128)} %multiply_add_fusion.2), channel_id=1, source_target_pairs={{0,8},{8,16},{16,24},{24,32},{32,40},{40,48},{48,56},{56,64},{64,7... | collective-permute-start | bytes 786440 | tf_op jit(solution)/shard_map/while/body/eval_jaxpr/ppermute | solution.py:23
  396.4 12.8 %collective-permute-start = (f32[8,128,64]{2,1,0:T(8,128)}, f32[8,128,64]{2,1,0:T(8,128)S(1)}, u32[]{:S(2)}, u32[]{:S(2)}) collective-permute-start(f32[8,128,64]{2,1,0:T(8,128)} %multiply_add_fusion.2), channel_id=1, source_target_pairs={{0,8},{8,16},{16,24},{24,32},{32,40},{40,48},{48,56},{56,64},{64,7... | collective-permute-start | bytes 786440 | tf_op jit(solution)/shard_map/while/body/eval_jaxpr/ppermute | solution.py:23
  410.2 12.0 %collective-permute-start = (f32[8,128,64]{2,1,0:T(8,128)}, f32[8,128,64]{2,1,0:T(8,128)S(1)}, u32[]{:S(2)}, u32[]{:S(2)}) collective-permute-start(f32[8,128,64]{2,1,0:T(8,128)} %multiply_add_fusion.2), channel_id=1, source_target_pairs={{0,8},{8,16},{16,24},{24,32},{32,40},{40,48},{48,56},{56,64},{64,7... | collective-permute-start | bytes 786440 | tf_op jit(solution)/shard_map/while/body/eval_jaxpr/ppermute | solution.py:23
  423.1 11.6 %collective-permute-start = (f32[8,128,64]{2,1,0:T(8,128)}, f32[8,128,64]{2,1,0:T(8,128)S(1)}, u32[]{:S(2)}, u32[]{:S(2)}) collective-permute-start(f32[8,128,64]{2,1,0:T(8,128)} %multiply_add_fusion.2), channel_id=1, source_target_pairs={{0,8},{8,16},{16,24},{24,32},{32,40},{40,48},{48,56},{56,64},{64,7... | collective-permute-start | bytes 786440 | tf_op jit(solution)/shard_map/while/body/eval_jaxpr/ppermute | solution.py:23
  435.6 11.6 %collective-permute-start = (f32[8,128,64]{2,1,0:T(8,128)}, f32[8,128,64]{2,1,0:T(8,128)S(1)}, u32[]{:S(2)}, u32[]{:S(2)}) collective-permute-start(f32[8,128,64]{2,1,0:T(8,128)} %multiply_add_fusion.2), channel_id=1, source_target_pairs={{0,8},{8,16},{16,24},{24,32},{32,40},{40,48},{48,56},{56,64},{64,7... | collective-permute-start | bytes 786440 | tf_op jit(solution)/shard_map/while/body/eval_jaxpr/ppermute | solution.py:23
  448.1 11.7 %collective-permute-start = (f32[8,128,64]{2,1,0:T(8,128)}, f32[8,128,64]{2,1,0:T(8,128)S(1)}, u32[]{:S(2)}, u32[]{:S(2)}) collective-permute-start(f32[8,128,64]{2,1,0:T(8,128)} %multiply_add_fusion.2), channel_id=1, source_target_pairs={{0,8},{8,16},{16,24},{24,32},{32,40},{40,48},{48,56},{56,64},{64,7... | collective-permute-start | bytes 786440 | tf_op jit(solution)/shard_map/while/body/eval_jaxpr/ppermute | solution.py:23
  460.7 12.5 %collective-permute-start = (f32[8,128,64]{2,1,0:T(8,128)}, f32[8,128,64]{2,1,0:T(8,128)S(1)}, u32[]{:S(2)}, u32[]{:S(2)}) collective-permute-start(f32[8,128,64]{2,1,0:T(8,128)} %multiply_add_fusion.2), channel_id=1, source_target_pairs={{0,8},{8,16},{16,24},{24,32},{32,40},{40,48},{48,56},{56,64},{64,7... | collective-permute-start | bytes 786440 | tf_op jit(solution)/shard_map/while/body/eval_jaxpr/ppermute | solution.py:23
  474.2 14.0 %collective-permute-start = (f32[8,128,64]{2,1,0:T(8,128)}, f32[8,128,64]{2,1,0:T(8,128)S(1)}, u32[]{:S(2)}, u32[]{:S(2)}) collective-permute-start(f32[8,128,64]{2,1,0:T(8,128)} %multiply_add_fusion.2), channel_id=1, source_target_pairs={{0,8},{8,16},{16,24},{24,32},{32,40},{40,48},{48,56},{56,64},{64,7... | collective-permute-start | bytes 786440 | tf_op jit(solution)/shard_map/while/body/eval_jaxpr/ppermute | solution.py:23
  489.1 15.3 %collective-permute-start = (f32[8,128,64]{2,1,0:T(8,128)}, f32[8,128,64]{2,1,0:T(8,128)S(1)}, u32[]{:S(2)}, u32[]{:S(2)}) collective-permute-start(f32[8,128,64]{2,1,0:T(8,128)} %multiply_add_fusion.2), channel_id=1, source_target_pairs={{0,8},{8,16},{16,24},{24,32},{32,40},{40,48},{48,56},{56,64},{64,7... | collective-permute-start | bytes 786440 | tf_op jit(solution)/shard_map/while/body/eval_jaxpr/ppermute | solution.py:23
  505.3 14.7 %collective-permute-start = (f32[8,128,64]{2,1,0:T(8,128)}, f32[8,128,64]{2,1,0:T(8,128)S(1)}, u32[]{:S(2)}, u32[]{:S(2)}) collective-permute-start(f32[8,128,64]{2,1,0:T(8,128)} %multiply_add_fusion.2), channel_id=1, source_target_pairs={{0,8},{8,16},{16,24},{24,32},{32,40},{40,48},{48,56},{56,64},{64,7... | collective-permute-start | bytes 786440 | tf_op jit(solution)/shard_map/while/body/eval_jaxpr/ppermute | solution.py:23
  520.9 15.9 %collective-permute-start = (f32[8,128,64]{2,1,0:T(8,128)}, f32[8,128,64]{2,1,0:T(8,128)S(1)}, u32[]{:S(2)}, u32[]{:S(2)}) collective-permute-start(f32[8,128,64]{2,1,0:T(8,128)} %multiply_add_fusion.2), channel_id=1, source_target_pairs={{0,8},{8,16},{16,24},{24,32},{32,40},{40,48},{48,56},{56,64},{64,7... | collective-permute-start | bytes 786440 | tf_op jit(solution)/shard_map/while/body/eval_jaxpr/ppermute | solution.py:23
  537.7 15.7 %collective-permute-start = (f32[8,128,64]{2,1,0:T(8,128)}, f32[8,128,64]{2,1,0:T(8,128)S(1)}, u32[]{:S(2)}, u32[]{:S(2)}) collective-permute-start(f32[8,128,64]{2,1,0:T(8,128)} %multiply_add_fusion.2), channel_id=1, source_target_pairs={{0,8},{8,16},{16,24},{24,32},{32,40},{40,48},{48,56},{56,64},{64,7... | collective-permute-start | bytes 786440 | tf_op jit(solution)/shard_map/while/body/eval_jaxpr/ppermute | solution.py:23
  554.4 19.0 %collective-permute-start = (f32[8,128,64]{2,1,0:T(8,128)}, f32[8,128,64]{2,1,0:T(8,128)S(1)}, u32[]{:S(2)}, u32[]{:S(2)}) collective-permute-start(f32[8,128,64]{2,1,0:T(8,128)} %multiply_add_fusion.2), channel_id=1, source_target_pairs={{0,8},{8,16},{16,24},{24,32},{32,40},{40,48},{48,56},{56,64},{64,7... | collective-permute-start | bytes 786440 | tf_op jit(solution)/shard_map/while/body/eval_jaxpr/ppermute | solution.py:23
  574.2 17.8 %collective-permute-start = (f32[8,128,64]{2,1,0:T(8,128)}, f32[8,128,64]{2,1,0:T(8,128)S(1)}, u32[]{:S(2)}, u32[]{:S(2)}) collective-permute-start(f32[8,128,64]{2,1,0:T(8,128)} %multiply_add_fusion.2), channel_id=1, source_target_pairs={{0,8},{8,16},{16,24},{24,32},{32,40},{40,48},{48,56},{56,64},{64,7... | collective-permute-start | bytes 786440 | tf_op jit(solution)/shard_map/while/body/eval_jaxpr/ppermute | solution.py:23
  593.0 15.9 %collective-permute-start = (f32[8,128,64]{2,1,0:T(8,128)}, f32[8,128,64]{2,1,0:T(8,128)S(1)}, u32[]{:S(2)}, u32[]{:S(2)}) collective-permute-start(f32[8,128,64]{2,1,0:T(8,128)} %multiply_add_fusion.2), channel_id=1, source_target_pairs={{0,8},{8,16},{16,24},{24,32},{32,40},{40,48},{48,56},{56,64},{64,7... | collective-permute-start | bytes 786440 | tf_op jit(solution)/shard_map/while/body/eval_jaxpr/ppermute | solution.py:23
  609.8 13.7 %collective-permute-start = (f32[8,128,64]{2,1,0:T(8,128)}, f32[8,128,64]{2,1,0:T(8,128)S(1)}, u32[]{:S(2)}, u32[]{:S(2)}) collective-permute-start(f32[8,128,64]{2,1,0:T(8,128)} %multiply_add_fusion.2), channel_id=1, source_target_pairs={{0,8},{8,16},{16,24},{24,32},{32,40},{40,48},{48,56},{56,64},{64,7... | collective-permute-start | bytes 786440 | tf_op jit(solution)/shard_map/while/body/eval_jaxpr/ppermute | solution.py:23
  624.4 12.0 %collective-permute-start = (f32[8,128,64]{2,1,0:T(8,128)}, f32[8,128,64]{2,1,0:T(8,128)S(1)}, u32[]{:S(2)}, u32[]{:S(2)}) collective-permute-start(f32[8,128,64]{2,1,0:T(8,128)} %multiply_add_fusion.2), channel_id=1, source_target_pairs={{0,8},{8,16},{16,24},{24,32},{32,40},{40,48},{48,56},{56,64},{64,7... | collective-permute-start | bytes 786440 | tf_op jit(solution)/shard_map/while/body/eval_jaxpr/ppermute | solution.py:23
  637.3 11.5 %collective-permute-start = (f32[8,128,64]{2,1,0:T(8,128)}, f32[8,128,64]{2,1,0:T(8,128)S(1)}, u32[]{:S(2)}, u32[]{:S(2)}) collective-permute-start(f32[8,128,64]{2,1,0:T(8,128)} %multiply_add_fusion.2), channel_id=1, source_target_pairs={{0,8},{8,16},{16,24},{24,32},{32,40},{40,48},{48,56},{56,64},{64,7... | collective-permute-start | bytes 786440 | tf_op jit(solution)/shard_map/while/body/eval_jaxpr/ppermute | solution.py:23
  649.8 11.4 %collective-permute-start = (f32[8,128,64]{2,1,0:T(8,128)}, f32[8,128,64]{2,1,0:T(8,128)S(1)}, u32[]{:S(2)}, u32[]{:S(2)}) collective-permute-start(f32[8,128,64]{2,1,0:T(8,128)} %multiply_add_fusion.2), channel_id=1, source_target_pairs={{0,8},{8,16},{16,24},{24,32},{32,40},{40,48},{48,56},{56,64},{64,7... | collective-permute-start | bytes 786440 | tf_op jit(solution)/shard_map/while/body/eval_jaxpr/ppermute | solution.py:23
  (33 other events, 1160.9 us)
Sparse Core Ops, SparseCore 0:
  9.9 75.4 all-gather.6
  88.1 80.3 all-gather.4
  171.0 75.2 all-gather.8
  753.7 72.7 reduce-scatter.1
